TPU v7x, 256 devices: a whole 4x4x8 slice. The times are simulated.
256 devices in a mesh: ta: 8 (over x_lo, y), gx: 4 (over x_hi, core), yz: 8 (over z).
Axes of the slice: x: 4 (x_hi: 2, x_lo: 2; x = x_hi * 2 + x_lo), y: 4, z: 8, core: 2. Of those that a mesh axis runs over, the one named last changes fastest.
Arguments:
- vectors: bfloat16 [2, 3, 32, 64, 256, 128], P(None, None, 'gx', 'yz', 'ta'), parts along dimension 4, may hold values from -6 to 6
- gauge_x: float32 [2, 3, 3, 32, 64, 256], P(None, None, None, 'gx', 'yz', 'ta'), parts along dimension 5, may hold values from -6 to 6
- gauge_y: float32 [2, 3, 3, 32, 64, 256], P(None, None, None, 'gx', 'yz', 'ta'), parts along dimension 5, may hold values from -6 to 6
Outputs:
- elementals: float32 [16, 2, 128, 128], P('ta'), parts along dimension 0
There are 8 independent parts, one for each index of `ta`. A program takes and returns all parts, laid end to end along the dimension named above; each array names one. Nothing has to cross between parts.
All inputs are finite; a program needn't handle non-finite values.
Results may differ from a plain program's by a relative error of at most 0.0029.
Values may be sent and summed in bfloat16 or wider, within the bound.
No kernel may reach another device: no remote copies, remote signals or barrier semaphores. Data moves between devices by JAX's collectives and lax.ppermute only.
A program may use at most 64 MiB of HBM per device.

v0:
```python
import math
import jax
import jax.numpy as jnp
from jax import lax
from jax.sharding import PartitionSpec as P


def shifted(value, axis, steps):
    count = lax.axis_size(axis)
    pairs = [(source, (source + steps) % count) for source in range(count)]
    return lax.ppermute(value, axis, pairs)


def colour_apply(gauge, source_vectors):
    real_parts = []
    imag_parts = []
    for colour in range(3):
        real_running = jnp.zeros(source_vectors.shape[2:], jnp.float32)
        imaginary_running = jnp.zeros(source_vectors.shape[2:], jnp.float32)
        for inner_product in range(3):
            left_real = gauge[0, colour, inner_product][..., None]
            left_imaginary = gauge[1, colour, inner_product][..., None]
            right_real = source_vectors[0, inner_product].astype(jnp.float32)
            right_imaginary = source_vectors[1, inner_product].astype(jnp.float32)
            real_running = real_running + left_real * right_real - left_imaginary * right_imaginary
            imaginary_running = (
                imaginary_running + left_real * right_imaginary + left_imaginary * right_real
            )
        real_parts.append(real_running)
        imag_parts.append(imaginary_running)
    return jnp.stack([jnp.stack(real_parts), jnp.stack(imag_parts)]).astype(jnp.bfloat16)


def right_block(image):
    nvecs = image.shape[-1]
    real_rows = image[0].reshape(-1, nvecs)
    imag_rows = image[1].reshape(-1, nvecs)
    first = jnp.concatenate([real_rows, imag_rows], 0)
    second = jnp.concatenate([imag_rows, -real_rows], 0)
    return (first, second)


def contract(left_cols, right_cols):
    return lax.dot_general(
        left_cols, right_cols, (((0,), (0,)), ((), ())), preferred_element_type=jnp.float32
    )


def local(vectors, gauge_x, gauge_y):
    nvecs = vectors.shape[-1]
    from_next_x = shifted(vectors[:, :, :1], "gx", -1)
    shifted_x = jnp.concatenate([vectors[:, :, 1:], from_next_x], 2)
    from_next_y = shifted(vectors[:, :, :, :1], "yz", -1)
    shifted_y = jnp.concatenate([vectors[:, :, :, 1:], from_next_y], 3)
    image_x = colour_apply(gauge_x, shifted_x)
    image_y = colour_apply(gauge_y, shifted_y)
    left_rows = vectors.reshape(-1, nvecs)
    blocks = right_block(image_x) + right_block(image_y)
    summed = lax.psum(
        jnp.concatenate([contract(left_rows, member) for member in blocks], 1), ("gx", "yz")
    )
    sites_total = (
        vectors.shape[2]
        * lax.axis_size("gx")
        * vectors.shape[3]
        * lax.axis_size("yz")
        * vectors.shape[4]
    )
    scaling = 1.0 / math.sqrt(3.0 * sites_total)
    return (summed * scaling).reshape(nvecs, 2, 2, nvecs).transpose(1, 2, 0, 3)


def solution(mesh):
    placed = (
        P(None, None, "gx", "yz", "ta", None),
        P(None, None, None, "gx", "yz", "ta"),
        P(None, None, None, "gx", "yz", "ta"),
    )
    return jax.shard_map(
        local, mesh=mesh, in_specs=placed, out_specs=P("ta", None, None, None), check_vma=False
    )
```

profile of v0, /device:TPU:8, one launch (start us, length us, event | category | flops | bytes accessed | tf_op | source)
XLA Modules:
  0.0 315.3 jit_solution(16234775033811610859)
XLA Ops:
  6.5 0.0 all-reduce.2.cloned.1.call-start
  6.5 1.0 slice.186
  7.6 0.0 copy-start
  7.6 2.5 collective-permute-start
  10.1 1.0 slice.212
  11.1 5.9 %collective-permute-start.1 = (bf16[2,3,8,1,32,128]{5,4,3,2,1,0:T(8,128)(2,1)S(1)}, bf16[2,3,8,1,32,128]{5,4,3,2,1,0:T(8,128)(2,1)S(1)}, u32[]{:S(2)}, u32[]{:S(2)}) collective-permute-start(bf16[2,3,8,1,32,128]{5,4,3,2,1,0:T(8,128)(2,1)S(1)} %slice.212), channel_id=1, source_target_pairs={{0,7},{1,0},{2,1},{3,2},{4,3},{5,4},{6,5},{7,6},{8,15},{9,8},{10,9... | collective-permute-start | bytes 1179656 | tf_op jit(solution)/shard_map/ppermute | solution.py:11
  17.1 0.0 copy-done
  17.1 0.7 slice.211
  17.8 0.4 copy-done.1
  18.2 0.1 copy-done.2
  18.4 0.0 collective-permute-done
  18.4 0.8 slice-done
  19.2 2.1 fusion.51
  21.3 1.9 fusion.33
  23.3 3.9 %fusion.57 = (bf16[1,8,8,32,128]{4,3,2,1,0:T(8,128)(2,1)S(1)}, bf16[1,8,8,32,128]{4,3,2,1,0:T(8,128)(2,1)S(1)}, bf16[1,8,8,32,128]{4,3,2,1,0:T(8,128)(2,1)S(1)}, bf16[1,8,8,32,128]{4,3,2,1,0:T(8,128)(2,1)S(1)}) fusion(bf16[1,8,8,32,128]{4,3,2,1,0:T(8,128)(2,1)S(1)} %get-tuple-element.11, bf16[1,8,8,32,128]{4,3,2,1,0:T(8,128)(2,1)S(1)} %get-tuple-element.10, ...), kind=kLoop, calls=%fused_computation.145 | loop fusion | flops 14155776 | bytes 5341184 | tf_op jit(solution)/shard_map/convert.26
  27.2 0.3 pad_maximum_fusion
  27.5 0.3 bitcast_negate_fusion.1
  27.8 1.0 fusion.25
  28.9 1.0 fusion.22
  29.9 0.0 collective-permute-done.1
  29.9 2.0 fusion.87
  31.9 1.9 fusion.69
  33.9 3.9 %fusion.93 = (bf16[1,8,8,32,128]{4,3,2,1,0:T(8,128)(2,1)S(1)}, bf16[1,8,8,32,128]{4,3,2,1,0:T(8,128)(2,1)S(1)}, bf16[1,8,8,32,128]{4,3,2,1,0:T(8,128)(2,1)S(1)}, bf16[1,8,8,32,128]{4,3,2,1,0:T(8,128)(2,1)S(1)}) fusion(bf16[1,8,8,32,128]{4,3,2,1,0:T(8,128)(2,1)S(1)} %get-tuple-element.18, bf16[1,8,8,32,128]{4,3,2,1,0:T(8,128)(2,1)S(1)} %get-tuple-element.17, ...), kind=kLoop, calls=%fused_computation.181 | loop fusion | flops 14155776 | bytes 5341184 | tf_op jit(solution)/shard_map/convert.16
  37.8 0.3 pad_maximum_fusion.2
  38.2 0.3 bitcast_negate_fusion
  38.5 1.0 fusion.19
  39.5 1.1 fusion.16
  40.6 0.7 pad_maximum_fusion.6
  41.3 0.0 all-reduce.2.cloned.1.call-update
  41.3 265.3 %all-reduce.2.cloned.1.call-done = f32[128,512]{0,1:T(8,128)} async-done(((f32[128,512]{0,1:T(8,128)}), f32[128,512]{0,1:T(8,128)}) %all-reduce.2.cloned.1.call-update) | async-done | bytes 262160 | tf_op jit(solution)/shard_map/psum | solution.py:59
  306.6 1.0 broadcast_multiply_fusion
  307.6 0.8 copy.4
  (5 shorter events, 0.1 us)
Async XLA Ops:
  6.5 300.1 %all-reduce.2.cloned.1.call-start = ((), (), s32[]{:S(2)}) async-start(), calls=%async_computation | async-start | bytes 524288 | tf_op jit(solution)/shard_map/psum | solution.py:59
  7.6 9.5 %copy-start = (bf16[2,3,8,8,32,128]{5,4,3,2,1,0:T(8,128)(2,1)S(1)}, bf16[2,3,8,8,32,128]{5,4,3,2,1,0:T(8,128)(2,1)}, u32[]{:S(2)}) copy-start(bf16[2,3,8,8,32,128]{5,4,3,2,1,0:T(8,128)(2,1)} %param.3) | copy-start | bytes 9437188
  7.6 10.8 %collective-permute-start = (bf16[2,3,1,8,32,128]{5,4,3,2,1,0:T(8,128)(2,1)S(1)}, bf16[2,3,1,8,32,128]{5,4,3,2,1,0:T(8,128)(2,1)S(1)}, u32[]{:S(2)}, u32[]{:S(2)}) collective-permute-start(bf16[2,3,1,8,32,128]{5,4,3,2,1,0:T(8,128)(2,1)S(1)} %slice.186), channel_id=1, source_target_pairs={{0,24},{8,0},{16,8},{24,16},{1,25},{9,1},{17,9},{25,17},{2,26},{10... | collective-permute-start | bytes 1179656 | tf_op jit(solution)/shard_map/ppermute | solution.py:11
  11.1 18.8 %collective-permute-start.1 = (bf16[2,3,8,1,32,128]{5,4,3,2,1,0:T(8,128)(2,1)S(1)}, bf16[2,3,8,1,32,128]{5,4,3,2,1,0:T(8,128)(2,1)S(1)}, u32[]{:S(2)}, u32[]{:S(2)}) collective-permute-start(bf16[2,3,8,1,32,128]{5,4,3,2,1,0:T(8,128)(2,1)S(1)} %slice.212), channel_id=1, source_target_pairs={{0,7},{1,0},{2,1},{3,2},{4,3},{5,4},{6,5},{7,6},{8,15},{9,8},{10,9... | collective-permute-start | bytes 1179656 | tf_op jit(solution)/shard_map/ppermute | solution.py:11
  17.1 1.1 copy-start.1
  17.1 1.2 copy-start.2
  17.1 2.1 slice-start
Sparse Core Ops, SparseCore 0:
  41.5 265.1 all-reduce.1
where the time goes:
time: 315 us
  waiting for transfers between devices  265 us (84%)
  other arithmetic  18.8 us (6%)
  between operations  13.6 us (4%)
  starting transfers between devices  8.47 us (3%)
  local copies, waits for them, and re-layouts  5 us (2%)
  matrix products  4.18 us (1%)
    psum x1, waiting for transfers between devices, local(): lax.psum(jnp.concatenate([contract(left_rows, member) for member in block...  265 us
    another operation x6, other arithmetic  15.8 us
    ppermute x2, starting transfers between devices, shifted(): return lax.ppermute(value, axis, pairs)  8.47 us
  transfers between devices with their start and end apart: 3, of which 1 were waited for; matrix products, arithmetic and copies ran while one was open for 4% of the time, Pallas kernels for 0%

commit v1 on v0

--- a/solution.py
+++ b/solution.py
@@ -3,6 +3,12 @@
 import jax.numpy as jnp
 from jax import lax
 from jax.sharding import PartitionSpec as P
+
+
+def gather_and_add(shard, mesh_axis):
+    parts = lax.all_gather(shard, mesh_axis, axis=0, tiled=False)
+    total = parts.sum(axis=0)
+    return total
 
 
 def shifted(value, axis, steps):
@@ -56,7 +62,7 @@
     image_y = colour_apply(gauge_y, shifted_y)
     left_rows = vectors.reshape(-1, nvecs)
     blocks = right_block(image_x) + right_block(image_y)
-    summed = lax.psum(
+    summed = gather_and_add(
         jnp.concatenate([contract(left_rows, member) for member in blocks], 1), ("gx", "yz")
     )
     sites_total = (

time: 315 us -> 167 us (0.53)
  waiting for transfers between devices: 265 us -> 111 us
  local copies, waits for them, and re-layouts: 5 us -> 9.37 us
    psum x1 -> x0, waiting for transfers between devices: 265 us -> none  [local(): lax.psum(jnp.concatenate([contract(left_rows, member) for member in block...]
    all_gather x0 -> x1, waiting for transfers between devices: none -> 107 us  [gather_and_add(): parts = lax.all_gather(shard, mesh_axis, axis=0, tiled=False)]
    unnamed x6 -> x7, local copies, waits for them, and re-layouts: 0.49 us -> 5.7 us
    ppermute x2, waiting for transfers between devices: 0.01 us -> 4 us  [shifted(): return lax.ppermute(value, axis, pairs)]
  transfers between devices with their start and end apart: 3 -> 3, of which waited for: 1 -> 2; matrix products, arithmetic and copies ran while one was open for 4% -> 8% of each run, Pallas kernels for 0% -> 0%
where the time goes in v1:
time: 167 us; the launch traced here: 165 us
  waiting for transfers between devices  111 us (66%)
  other arithmetic  19.4 us (12%)
  between operations  13.6 us (8%)
  local copies, waits for them, and re-layouts  9.37 us (6%)
  starting transfers between devices  8.2 us (5%)
  matrix products  4.18 us (3%)
    all_gather x1, waiting for transfers between devices, gather_and_add(): parts = lax.all_gather(shard, mesh_axis, axis=0, tiled=False)  107 us
    another operation x6, other arithmetic  15.8 us
    ppermute x2, starting transfers between devices, shifted(): return lax.ppermute(value, axis, pairs)  8.19 us
    unnamed x7, local copies, waits for them, and re-layouts  5.7 us
    dot_general x4, matrix products, contract(): lax.dot_general(left_cols, right_cols, (((0,), (0,)), ((), ())), preferre...  4.18 us
    ppermute x2, waiting for transfers between devices, shifted(): return lax.ppermute(value, axis, pairs)  4 us
  transfers between devices with their start and end apart: 3, of which 2 were waited for; matrix products, arithmetic and copies ran while one was open for 8% of the time, Pallas kernels for 0%

profile of v1, /device:TPU:8, one launch (start us, length us, event | category | flops | bytes accessed | tf_op | source)
XLA Modules:
  0.0 165.4 jit_solution(16270096715547627542)
XLA Ops:
  6.5 0.0 all-gather.3.cloned.1.call-start
  6.5 1.0 slice.212
  7.6 0.0 copy-start
  7.6 5.9 %collective-permute-start.1 = (bf16[2,3,8,1,32,128]{5,4,3,2,1,0:T(8,128)(2,1)S(1)}, bf16[2,3,8,1,32,128]{5,4,3,2,1,0:T(8,128)(2,1)S(1)}, u32[]{:S(2)}, u32[]{:S(2)}) collective-permute-start(bf16[2,3,8,1,32,128]{5,4,3,2,1,0:T(8,128)(2,1)S(1)} %slice.212), channel_id=1, source_target_pairs={{0,7},{1,0},{2,1},{3,2},{4,3},{5,4},{6,5},{7,6},{8,15},{9,8},{10,9... | collective-permute-start | bytes 1179656 | tf_op jit(solution)/shard_map/ppermute | solution.py:17
  13.5 1.0 slice.186
  14.5 2.3 %collective-permute-start = (bf16[2,3,1,8,32,128]{5,4,3,2,1,0:T(8,128)(2,1)S(1)}, bf16[2,3,1,8,32,128]{5,4,3,2,1,0:T(8,128)(2,1)S(1)}, u32[]{:S(2)}, u32[]{:S(2)}) collective-permute-start(bf16[2,3,1,8,32,128]{5,4,3,2,1,0:T(8,128)(2,1)S(1)} %slice.186), channel_id=1, source_target_pairs={{0,24},{8,0},{16,8},{24,16},{1,25},{9,1},{17,9},{25,17},{2,26},{10... | collective-permute-start | bytes 1179656 | tf_op jit(solution)/shard_map/ppermute | solution.py:17
  16.8 0.7 slice.211
  17.5 0.4 copy-done.1
  17.9 0.1 copy-done.2
  18.1 4.0 %collective-permute-done = bf16[2,3,1,8,32,128]{5,4,3,2,1,0:T(8,128)(2,1)S(1)} collective-permute-done((bf16[2,3,1,8,32,128]{5,4,3,2,1,0:T(8,128)(2,1)S(1)}, bf16[2,3,1,8,32,128]{5,4,3,2,1,0:T(8,128)(2,1)S(1)}, u32[]{:S(2)}, u32[]{:S(2)}) %collective-permute-start) | collective-permute-done | bytes 393248 | tf_op jit(solution)/shard_map/ppermute | solution.py:17
  22.1 0.0 slice-done
  22.1 2.1 %fusion.51 = (bf16[1,8,8,32,128]{4,3,2,1,0:T(8,128)(2,1)S(1)}, bf16[1,8,8,32,128]{4,3,2,1,0:T(8,128)(2,1)S(1)}, bf16[1,8,8,32,128]{4,3,2,1,0:T(8,128)(2,1)S(1)},...) fusion(f32[8,8,32]{2,1,0:T(8,128)S(1)} %get-tuple-element.41, ...), kind=kLoop, calls=%fused_computation.140 | loop fusion | flops 6291456 | bytes 6864896 | tf_op jit(solution)/shard_map/convert.25
  24.2 1.9 %fusion.33 = bf16[1,8,8,32,128]{4,3,2,1,0:T(8,128)(2,1)S(1)} fusion(bf16[1,8,8,32,128]{4,3,2,1,0:T(8,128)(2,1)S(1)} %get-tuple-element.11, bf16[1,8,8,32,128]{4,3,2,1,0:T(8,128)(2,1)S(1)} %get-tuple-element.10, bf16[1,8,8,32,128]{4,3,2,1,0:T(8,128)(2,1)S(1)} %get-tuple-element.9, bf16[1,8,8,32,128]{4,3,2,1,0:T(8,128)(2,1)S(1)} %get-tuple-element.8, ...), kind=kLoop, calls=%fused_computation.122 | loop fusion | flops 4718592 | bytes 3719168 | tf_op jit(solution)/shard_map/convert.29
  26.1 3.9 %fusion.57 = (bf16[1,8,8,32,128]{4,3,2,1,0:T(8,128)(2,1)S(1)}, bf16[1,8,8,32,128]{4,3,2,1,0:T(8,128)(2,1)S(1)}, bf16[1,8,8,32,128]{4,3,2,1,0:T(8,128)(2,1)S(1)}, bf16[1,8,8,32,128]{4,3,2,1,0:T(8,128)(2,1)S(1)}) fusion(bf16[1,8,8,32,128]{4,3,2,1,0:T(8,128)(2,1)S(1)} %get-tuple-element.11, bf16[1,8,8,32,128]{4,3,2,1,0:T(8,128)(2,1)S(1)} %get-tuple-element.10, ...), kind=kLoop, calls=%fused_computation.146 | loop fusion | flops 14155776 | bytes 5341184 | tf_op jit(solution)/shard_map/convert.26
  30.0 0.3 pad_maximum_fusion
  30.4 0.3 bitcast_negate_fusion.1
  30.7 1.0 fusion.25
  31.8 1.0 fusion.22
  32.8 0.0 collective-permute-done.1
  32.8 2.0 %fusion.87 = (bf16[1,8,8,32,128]{4,3,2,1,0:T(8,128)(2,1)S(1)}, bf16[1,8,8,32,128]{4,3,2,1,0:T(8,128)(2,1)S(1)}, bf16[1,8,8,32,128]{4,3,2,1,0:T(8,128)(2,1)S(1)},...) fusion(f32[8,8,32]{2,1,0:T(8,128)S(1)} %get-tuple-element.59, ...), kind=kLoop, calls=%fused_computation.176 | loop fusion | flops 6291456 | bytes 6864896 | tf_op jit(solution)/shard_map/convert.15
  34.8 1.9 %fusion.69 = bf16[1,8,8,32,128]{4,3,2,1,0:T(8,128)(2,1)S(1)} fusion(bf16[1,8,8,32,128]{4,3,2,1,0:T(8,128)(2,1)S(1)} %get-tuple-element.18, bf16[1,8,8,32,128]{4,3,2,1,0:T(8,128)(2,1)S(1)} %get-tuple-element.17, bf16[1,8,8,32,128]{4,3,2,1,0:T(8,128)(2,1)S(1)} %get-tuple-element.16, bf16[1,8,8,32,128]{4,3,2,1,0:T(8,128)(2,1)S(1)} %get-tuple-element.15, ...), kind=kLoop, calls=%fused_computation.158 | loop fusion | flops 4718592 | bytes 3719168 | tf_op jit(solution)/shard_map/convert.19
  36.8 3.9 %fusion.93 = (bf16[1,8,8,32,128]{4,3,2,1,0:T(8,128)(2,1)S(1)}, bf16[1,8,8,32,128]{4,3,2,1,0:T(8,128)(2,1)S(1)}, bf16[1,8,8,32,128]{4,3,2,1,0:T(8,128)(2,1)S(1)}, bf16[1,8,8,32,128]{4,3,2,1,0:T(8,128)(2,1)S(1)}) fusion(bf16[1,8,8,32,128]{4,3,2,1,0:T(8,128)(2,1)S(1)} %get-tuple-element.18, bf16[1,8,8,32,128]{4,3,2,1,0:T(8,128)(2,1)S(1)} %get-tuple-element.17, ...), kind=kLoop, calls=%fused_computation.182 | loop fusion | flops 14155776 | bytes 5341184 | tf_op jit(solution)/shard_map/convert.16
  40.7 0.3 pad_maximum_fusion.2
  41.0 0.3 bitcast_negate_fusion
  41.4 1.0 fusion.19
  42.4 1.1 fusion.16
  43.5 0.7 pad_maximum_fusion.6
  44.2 0.0 all-gather.3.cloned.1.call-update
  44.2 106.7 %all-gather.3.cloned.1.call-done = f32[4096,512]{0,1:T(8,128)} async-done(((f32[128,512]{0,1:T(8,128)}), f32[4096,512]{0,1:T(8,128)}) %all-gather.3.cloned.1.call-update) | async-done | bytes 8388624 | tf_op jit(solution)/shard_map/all_gather | solution.py:9
  150.9 5.2 %copy.5 = f32[64,8,32,128]{3,2,1,0:T(8,128)S(1)} copy(f32[64,8,32,128]{3,1,2,0:T(8,128)} %bitcast.151) | data formatting | bytes 16777216
  156.1 1.6 bitcast_reduce_fusion
  157.7 0.8 copy.4
  (7 shorter events, 0.1 us)
Async XLA Ops:
  6.5 144.3 %all-gather.3.cloned.1.call-start = ((), (), s32[]{:S(2)}) async-start(), calls=%async_computation | async-start | bytes 8650752 | tf_op jit(solution)/shard_map/all_gather | solution.py:9
  7.6 9.2 %copy-start = (bf16[2,3,8,8,32,128]{5,4,3,2,1,0:T(8,128)(2,1)S(1)}, bf16[2,3,8,8,32,128]{5,4,3,2,1,0:T(8,128)(2,1)}, u32[]{:S(2)}) copy-start(bf16[2,3,8,8,32,128]{5,4,3,2,1,0:T(8,128)(2,1)} %param.3) | copy-start | bytes 9437188
  7.6 25.2 %collective-permute-start.1 = (bf16[2,3,8,1,32,128]{5,4,3,2,1,0:T(8,128)(2,1)S(1)}, bf16[2,3,8,1,32,128]{5,4,3,2,1,0:T(8,128)(2,1)S(1)}, u32[]{:S(2)}, u32[]{:S(2)}) collective-permute-start(bf16[2,3,8,1,32,128]{5,4,3,2,1,0:T(8,128)(2,1)S(1)} %slice.212), channel_id=1, source_target_pairs={{0,7},{1,0},{2,1},{3,2},{4,3},{5,4},{6,5},{7,6},{8,15},{9,8},{10,9... | collective-permute-start | bytes 1179656 | tf_op jit(solution)/shard_map/ppermute | solution.py:17
  14.5 7.6 %collective-permute-start = (bf16[2,3,1,8,32,128]{5,4,3,2,1,0:T(8,128)(2,1)S(1)}, bf16[2,3,1,8,32,128]{5,4,3,2,1,0:T(8,128)(2,1)S(1)}, u32[]{:S(2)}, u32[]{:S(2)}) collective-permute-start(bf16[2,3,1,8,32,128]{5,4,3,2,1,0:T(8,128)(2,1)S(1)} %slice.186), channel_id=1, source_target_pairs={{0,24},{8,0},{16,8},{24,16},{1,25},{9,1},{17,9},{25,17},{2,26},{10... | collective-permute-start | bytes 1179656 | tf_op jit(solution)/shard_map/ppermute | solution.py:17
  16.8 1.1 copy-start.1
  16.8 1.2 copy-start.2
  16.8 5.3 %slice-start = ((bf16[2,3,8,8,32,128]{5,4,3,2,1,0:T(8,128)(2,1)}), bf16[2,3,7,8,32,128]{5,4,3,2,1,0:T(8,128)(2,1)S(1)}, s32[]{:S(2)}) async-start(bf16[2,3,8,8,32,128]{5,4,3,2,1,0:T(8,128)(2,1)} %param.3), calls=%async_computation.1 | async-start | bytes 5505024 | tf_op jit(solution)/shard_map/slice | solution.py:58
Sparse Core Ops, SparseCore 0:
  44.3 106.4 all-gather.2
